TPU v7x, 128 devices: a whole 4x4x4 slice. The times are simulated.
128 devices in a mesh: dp: 8 (over x, core), table: 16 (over z, y).
Axes of the slice: x: 4, y: 4, z: 4, core: 2. Of those that a mesh axis runs over, the one named last changes fastest.
Arguments:
- user_table: bfloat16 [524288, 256], P(('dp', 'table')), may hold values from -6 to 6
- item_table: bfloat16 [524288, 256], P(('dp', 'table')), may hold values from -6 to 6
- hist_owner: int32 [262144, 1], P(('dp', 'table')), may hold values from 0 to 127; in each aligned block of 2048 rows (0 to 2047, 2048 to 4095, ...) at most 32 rows name the same one
- hist_row: int32 [262144], P(('dp', 'table')), may hold values from 0 to 4095
- hist_seg: int32 [128, 2048], P(('dp', 'table')), may hold values from 0 to 127, never falling along the last dimension, each value on 1 to 64 neighbouring positions
- hist_wix: int32 [262144], P(('dp', 'table')), may hold values from 0 to 63
- bag_weights: bfloat16 [64], replicated, may hold values from 0.099609375 to 1
- item_owner: int32 [16384, 1], P(('dp', 'table')), may hold values from 0 to 127; in each aligned block of 128 rows (0 to 127, 128 to 255, ...) at most 2 rows name the same one
- item_row: int32 [16384], P(('dp', 'table')), may hold values from 0 to 4095
- user_proj: bfloat16 [256, 256], replicated, may hold values from -0.375 to 0.375
- item_proj: bfloat16 [256, 256], replicated, may hold values from -0.375 to 0.375
- logit_scale: float32 [1], replicated, may hold values from 8 to 600
Outputs:
- user_grad: float32 [524288, 256], P(('dp', 'table'))
- item_grad: float32 [524288, 256], P(('dp', 'table'))
- user_proj_grad: float32 [256, 256], replicated
- item_proj_grad: float32 [256, 256], replicated
Inputs may be any that keep to these rules, and one draw needn't show every extreme that they name: `hist_owner`: among the 2048 history ids of one device, no owner is named more than 32 times; some owner exactly 32 times. `item_owner`: among the 128 samples of one device, no owner is named more than 2 times; some owner exactly 2 times. `hist_seg`: each row numbers 128 samples in order; each sample has 1 to 64 ids, one has exactly 64.
All inputs are finite; a program needn't handle non-finite values.
Results may differ from a plain program's by a relative error of at most 0.01.
The roundings to bfloat16 on the way count: a program that leaves them out, or rounds other values in their place, can miss the bound.
Values may be sent and summed in bfloat16 or wider, within the bound.
No kernel may reach another device: no remote copies, remote signals or barrier semaphores. Data moves between devices by JAX's collectives and lax.ppermute only.
A program may use at most 128 MiB of HBM per device.

v0:
```python
import jax
import jax.numpy as jnp
from jax import lax
from jax.sharding import PartitionSpec as P

EPS = 1e-06
AXES = ("dp", "table")


def tower(x, weight):
    u = jnp.dot(x, weight, preferred_element_type=jnp.float32)
    r = lax.rsqrt(jnp.sum(u * u, -1, keepdims=True) + EPS)
    return (u * r, r)


def slot_rank(owner, devices):
    onehot = (owner[:, None] == jnp.arange(devices, dtype=jnp.int32)[None, :]).astype(jnp.int32)
    before = jnp.cumsum(onehot, 0) - onehot
    return jnp.sum(before * onehot, 1)


def pick_rows(table, wanted):
    rows_dev = table.shape[0]
    flat = wanted.reshape(-1)
    onehot = (flat[:, None] == jnp.arange(rows_dev, dtype=jnp.int32)[None, :]).astype(table.dtype)
    picked = jnp.dot(onehot, table, preferred_element_type=jnp.float32).astype(table.dtype)
    return picked.reshape(wanted.shape + table.shape[1:])


def add_rows(rows_dev, wanted, values):
    flat = wanted.reshape(-1)
    onehot = (jnp.arange(rows_dev, dtype=jnp.int32)[:, None] == flat[None, :]).astype(values.dtype)
    return jnp.dot(onehot, values.reshape(flat.shape[0], -1), preferred_element_type=jnp.float32)


def exchange(x):
    return lax.all_to_all(x, AXES, split_axis=1, concat_axis=1, tiled=True)


def local(
    user_table,
    item_table,
    hist_owner,
    hist_row,
    hist_seg,
    hist_wix,
    bag_weights,
    item_owner,
    item_row,
    user_proj,
    item_proj,
    logit_scale,
):
    rows_dev, width = user_table.shape
    n_dp = lax.axis_size("dp")
    n_tab = lax.axis_size("table")
    devices = n_dp * n_tab
    tokens = hist_row.shape[0]
    samples = item_row.shape[0]
    cap = max(2, 2 * tokens // devices)
    cap_item = max(2, 2 * samples // devices)
    slots = cap + cap_item
    myself = lax.axis_index(AXES)
    entries = bag_weights.shape[0]
    segment = hist_seg[0]
    sample_ids = jnp.arange(samples, dtype=jnp.int32)
    owner = jnp.concatenate([hist_owner[:, 0], item_owner[:, 0]])
    rank = jnp.concatenate(
        [slot_rank(hist_owner[:, 0], devices), cap + slot_rank(item_owner[:, 0], devices)]
    )
    row = jnp.concatenate([hist_row, item_row])
    fields = jnp.stack(
        [
            row & 255,
            row >> 8,
            jnp.concatenate([segment, sample_ids]),
            jnp.concatenate([hist_wix, jnp.zeros((samples,), jnp.int32)]),
            jnp.ones_like(row),
        ]
    )
    by_owner = (owner[None, :] == jnp.arange(devices, dtype=jnp.int32)[:, None]).astype(
        jnp.bfloat16
    )
    planes = (fields.astype(jnp.bfloat16)[:, None, :] * by_owner[None, :, :]).reshape(
        -1, owner.shape[0]
    )
    by_rank = (rank[:, None] == jnp.arange(slots, dtype=jnp.int32)[None, :]).astype(jnp.bfloat16)
    table = jnp.dot(planes, by_rank, preferred_element_type=jnp.float32)
    table = table.astype(jnp.int32).reshape(fields.shape[0], devices, slots)
    table = jnp.transpose(table, (0, 2, 1)).reshape(fields.shape[0], slots * devices)
    slot_row = table[0] + 256 * table[1]
    slot_seg = table[2]
    slot_wix = table[3]
    filled = table[4] > 0
    req = jnp.where(filled, slot_row, rows_dev).reshape(slots, devices)
    is_user = jnp.arange(slots * devices, dtype=jnp.int32) < cap * devices
    want = exchange(req)
    user_want = want[:cap]
    goods_want = want[cap:]
    goods_back = exchange(pick_rows(item_table, goods_want))
    user_back = exchange(pick_rows(user_table, user_want))
    wts = jnp.sum(
        jnp.where(
            slot_wix[:, None] == jnp.arange(entries, dtype=jnp.int32)[None, :],
            bag_weights[None, :].astype(jnp.float32),
            0.0,
        ),
        1,
    ).astype(jnp.bfloat16)
    of_sample = filled[None, :] & (slot_seg[None, :] == sample_ids[:, None])
    item_pick = of_sample[:, cap * devices :].astype(jnp.bfloat16)
    item_emb = jnp.dot(
        item_pick, goods_back.reshape(-1, width), preferred_element_type=jnp.float32
    ).astype(jnp.bfloat16)
    vn, rv = tower(item_emb, item_proj)
    vh = vn.astype(jnp.bfloat16)
    vh_all = lax.all_gather(vh, AXES, axis=0, tiled=True)
    coef = jnp.where(
        of_sample[:, : cap * devices], wts[None, : cap * devices], jnp.zeros((), jnp.bfloat16)
    )
    numer = jnp.dot(coef, user_back.reshape(-1, width), preferred_element_type=jnp.float32)
    denom = jnp.sum(coef.astype(jnp.float32), 1)
    bag = (numer / denom[:, None]).astype(jnp.bfloat16)
    un, ru = tower(bag, user_proj)
    uh = un.astype(jnp.bfloat16)
    uh_all = lax.all_gather(uh, AXES, axis=0, tiled=True)
    scale = logit_scale[0]
    total = vh_all.shape[0]
    mine = myself * samples + sample_ids
    everyone = jnp.arange(total, dtype=jnp.int32)
    scores = scale * jnp.dot(uh, vh_all.T, preferred_element_type=jnp.float32)
    top = jnp.max(scores, -1)
    expo = jnp.exp(scores - top[:, None])
    norm = jnp.sum(expo, -1)
    prob = expo / norm[:, None]
    hot = (everyone[None, :] == mine[:, None]).astype(jnp.float32)
    pw = (prob - hot).astype(jnp.bfloat16)
    d_un = scale / total * jnp.dot(pw, vh_all, preferred_element_type=jnp.float32)
    d_u = ru * (d_un - un * jnp.sum(un * d_un, -1, keepdims=True))
    highest = lax.Precision.HIGHEST
    user_part = jnp.dot(bag.astype(jnp.float32).T, d_u, precision=highest)
    d_bag = jnp.dot(d_u, user_proj.astype(jnp.float32).T, precision=highest)
    n_user = cap * devices
    pick = jnp.concatenate([d_bag, denom[:, None]], axis=1)
    per_slot = jnp.dot(of_sample[:, :n_user].T.astype(jnp.float32), pick, precision=highest)
    g_slot = (wts[:n_user].astype(jnp.float32) / per_slot[:, width])[:, None] * per_slot[:, :width]
    g_slot = jnp.where(filled[:n_user, None], g_slot, 0.0)
    got_user = exchange(g_slot.astype(jnp.bfloat16).reshape(cap, devices, width))
    user_grad = add_rows(rows_dev, user_want, got_user)
    stats = jnp.concatenate([top, norm]).reshape(1, 1, -1)
    stats = jnp.broadcast_to(stats, (devices, 1, stats.shape[-1]))
    stats = jnp.pad(stats, ((0, 0), (0, 0), (0, -stats.shape[-1] % width)))
    stats = stats.reshape(devices, -1, width)
    user_parts = jnp.transpose(user_part.reshape(-1, devices, width), (1, 0, 2))
    n_stat = stats.shape[1]
    got_s = lax.all_to_all(
        jnp.concatenate([stats, user_parts], axis=1), AXES, split_axis=0, concat_axis=0, tiled=True
    )
    flat_stats = got_s[:, :n_stat].reshape(devices, -1)
    top_all = flat_stats[:, :samples].reshape(total)
    norm_all = flat_stats[:, samples : 2 * samples].reshape(total)
    user_red = jnp.sum(got_s[:, n_stat:], 0)
    scores_c = scale * jnp.dot(vh, uh_all.T, preferred_element_type=jnp.float32)
    prob_c = jnp.exp(scores_c - top_all[None, :]) * (1.0 / norm_all)[None, :]
    hot_c = (everyone[None, :] == mine[:, None]).astype(jnp.float32)
    pw_c = (prob_c - hot_c).astype(jnp.bfloat16)
    d_vn = scale / total * jnp.dot(pw_c, uh_all, preferred_element_type=jnp.float32)
    d_v = rv * (d_vn - vn * jnp.sum(vn * d_vn, -1, keepdims=True))
    goods_part = jnp.dot(item_emb.astype(jnp.float32).T, d_v, precision=highest)
    d_v_slot = jnp.dot(item_pick.T.astype(jnp.float32), d_v, precision=highest)
    goods_parts = goods_part.reshape(-1, devices, width)
    chunk = goods_parts.shape[0]
    hi = goods_parts.astype(jnp.bfloat16)
    lo = (goods_parts - hi.astype(jnp.float32)).astype(jnp.bfloat16)
    send = jnp.concatenate(
        [d_v_slot.astype(jnp.bfloat16).reshape(cap_item, devices, width), hi, lo], axis=0
    )
    got = exchange(send)
    tail = got[cap_item:].astype(jnp.float32)
    goods_red = jnp.sum(tail[:chunk] + tail[chunk:], 1)
    red = jnp.concatenate([user_red, goods_red])
    spread = exchange(jnp.broadcast_to(red[:, None], (red.shape[0], devices, width)))
    user_proj_grad = spread[:chunk].reshape(width, width)
    item_proj_grad = spread[chunk:].reshape(width, width)
    item_grad = add_rows(rows_dev, goods_want, got[:cap_item])
    return (user_grad, item_grad, user_proj_grad, item_proj_grad)


def solution(mesh):
    in_specs = (
        P(AXES, None),
        P(AXES, None),
        P(AXES, None),
        P(AXES),
        P(AXES, None),
        P(AXES),
        P(),
        P(AXES, None),
        P(AXES),
        P(),
        P(),
        P(),
    )
    out_specs = (P(AXES, None), P(AXES, None), P(), P())
    return jax.shard_map(local, mesh=mesh, in_specs=in_specs, out_specs=out_specs, check_vma=False)
```

profile of v0, /device:TPU:1, one launch (start us, length us, event | category | flops | bytes accessed | tf_op | source)
XLA Modules:
  0.0 283.7 jit_solution(170055418482812964)
XLA Ops:
  7.2 0.9 fusion.47
  8.1 0.7 pad_add_fusion
  8.9 0.7 convert_reduce_fusion.1
  9.7 0.7 convert.27
  10.6 0.8 select_reduce_fusion.1
  11.4 0.8 copy.70
  12.2 0.3 fusion.34
  12.6 1.0 copy-done.4
  13.6 1.3 broadcast_add_fusion
  14.9 0.3 copy.71
  15.2 0.6 fusion.33
  16.0 0.3 broadcast_multiply_fusion
  16.3 1.2 convolution_convert_fusion.1
  17.7 0.7 copy.72
  18.5 11.5 %all-to-all-start = ((s32[34,128,1]{0,2,1:T(1,128)}), s32[34,128,1]{0,2,1:T(1,128)S(1)}, u32[]{:S(2)}, u32[]{:S(2)}) async-start(s32[34,128,1]{0,2,1:T(1,128)} %copy.72), calls=%async_computation | async-start | bytes 131072 | tf_op jit(solution)/shard_map/all_to_all | solution.py:37
  30.0 9.7 %all-to-all-done = s32[34,128,1]{0,2,1:T(1,128)S(1)} async-done(((s32[34,128,1]{0,2,1:T(1,128)}), s32[34,128,1]{0,2,1:T(1,128)S(1)}, u32[]{:S(2)}, u32[]{:S(2)}) %all-to-all-start) | async-done | bytes 17440 | tf_op jit(solution)/shard_map/all_to_all | solution.py:37
  40.0 2.4 fusion.25
  42.3 0.8 copy.77
  43.1 4.3 %all-to-all-start.2 = ((bf16[2,128,256]{2,0,1:T(2,128)(2,1)}), bf16[2,128,256]{2,0,1:T(2,128)(2,1)S(1)}, u32[]{:S(2)}, u32[]{:S(2)}) async-start(bf16[2,128,256]{2,0,1:T(2,128)(2,1)} %copy.77), calls=%async_computation.2 | async-start | bytes 262144 | tf_op jit(solution)/shard_map/all_to_all | solution.py:37
  47.4 0.3 all-gather.3.cloned.1.call-start
  47.8 0.4 fusion.18
  48.1 9.5 %all-to-all-done.2 = bf16[2,128,256]{2,0,1:T(2,128)(2,1)S(1)} async-done(((bf16[2,128,256]{2,0,1:T(2,128)(2,1)}), bf16[2,128,256]{2,0,1:T(2,128)(2,1)S(1)}, u32[]{:S(2)}, u32[]{:S(2)}) %all-to-all-start.2) | async-done | bytes 131104 | tf_op jit(solution)/shard_map/all_to_all | solution.py:37
  58.1 0.7 multiply_convert_fusion
  58.9 12.3 %fusion.11 = bf16[4096,256]{1,0:T(8,128)(2,1)S(1)} fusion(bf16[4096,256]{1,0:T(8,128)(2,1)S(1)} %copy-done, s32[4096]{0:T(1024)S(1)} %bitcast.105), kind=kOutput, calls=%fused_computation.18 | convolution fusion | flops 8607760384 | bytes 4210688 | tf_op jit(solution)/shard_map/dot_general | solution.py:26
  71.2 2.5 copy.74
  73.7 4.0 %all-to-all-start.1 = ((bf16[32,128,256]{2,0,1:T(8,128)(2,1)}), bf16[32,128,256]{2,0,1:T(8,128)(2,1)S(1)}, u32[]{:S(2)}, u32[]{:S(2)}) async-start(bf16[32,128,256]{2,0,1:T(8,128)(2,1)} %copy.74), calls=%async_computation.1 | async-start | bytes 4194304 | tf_op jit(solution)/shard_map/all_to_all | solution.py:37
  77.7 0.6 all-gather.5.cloned.1.call-start
  78.6 0.5 convert_reduce_fusion
  79.1 30.2 %all-to-all-done.1 = bf16[32,128,256]{2,0,1:T(8,128)(2,1)S(1)} async-done(((bf16[32,128,256]{2,0,1:T(8,128)(2,1)}), bf16[32,128,256]{2,0,1:T(8,128)(2,1)S(1)}, u32[]{:S(2)}, u32[]{:S(2)}) %all-to-all-start.1) | async-done | bytes 2097184 | tf_op jit(solution)/shard_map/all_to_all | solution.py:37
  109.4 1.2 copy.75
  110.5 0.7 fusion.30
  111.5 0.7 multiply_convert_fusion.1
  113.1 22.4 %all-gather.3.cloned.1.call-done = bf16[16384,256]{1,0:T(8,128)(2,1)} async-done(((bf16[128,256]{1,0:T(8,128)(2,1)}), bf16[16384,256]{1,0:T(8,128)(2,1)}) %all-gather.3.cloned.1.call-update) | async-done | bytes 8388624 | tf_op jit(solution)/shard_map/all_gather | solution.py:117
  135.5 6.3 %fusion.57 = (f32[128]{0:T(128)S(1)}, f32[128,16384]{1,0:T(8,128)S(1)}) fusion(bf16[128,256]{1,0:T(8,128)(2,1)} %multiply_convert_fusion.1, bf16[16384,256]{1,0:T(8,128)(2,1)} %all-gather.3.cloned.1.call-done, f32[]{:T(128)} %bitcast.78), kind=kOutput, calls=%fused_computation.123 | convolution fusion | flops 1077936000 | bytes 16843268 | tf_op jit(solution)/shard_map/dot_general | solution.py:131
  141.8 1.6 fusion.10
  143.4 1.8 copy-done.3
  145.2 2.9 %multiply_reduce_fusion.1 = (f32[128]{0:T(128)S(1)}, f32[128,256]{1,0:T(8,128)S(1)}) fusion(f32[128,256]{1,0:T(8,128)S(1)} %get-tuple-element.19, f32[128]{0:T(128)S(1)} %add_rsqrt_fusion.1, bf16[16384,256]{1,0:T(8,128)(2,1)S(1)} %copy-done.3, f32[128,16384]{1,0:T(8,128)S(1)} %get-tuple-element.21, s32[128]{0:T(128)S(1)} %iota_add_fusion, ...), kind=kOutput, calls=%fused_computation.79 | convolution fusion | flops 1086455680 | bytes 17041924 | tf_op jit(solution)/shard_map/dot_general | solution.py:138
  148.1 0.3 fusion.54
  148.5 2.0 fusion.22
  150.4 2.0 copy-done.2
  152.4 0.4 fusion.53
  153.1 1.0 pad_maximum_fusion
  154.2 5.4 %all-to-all-start.4 = ((f32[128,3,256]{2,1,0:T(4,128)}), f32[128,3,256]{2,1,0:T(4,128)S(1)}, u32[]{:S(2)}, u32[]{:S(2)}) async-start(f32[128,3,256]{2,1,0:T(4,128)} %pad_maximum_fusion), calls=%async_computation.4 | async-start | bytes 1048576 | tf_op jit(solution)/shard_map/all_to_all | solution.py:156
  159.6 2.8 fusion.19
  162.4 0.5 copy.94
  162.9 3.4 %copy.80 = bf16[32,128,256]{2,0,1:T(8,128)(2,1)} copy(bf16[32,128,256]{1,0,2:T(8,128)(2,1)S(1)} %bitcast.81) | data formatting | bytes 4194304 | tf_op jit(solution)/shard_map/reshape | solution.py:148
  166.3 7.3 %all-to-all-done.4 = f32[128,3,256]{2,1,0:T(4,128)S(1)} async-done(((f32[128,3,256]{2,1,0:T(4,128)}), f32[128,3,256]{2,1,0:T(4,128)S(1)}, u32[]{:S(2)}, u32[]{:S(2)}) %all-to-all-start.4) | async-done | bytes 393248 | tf_op jit(solution)/shard_map/all_to_all | solution.py:156
  173.6 4.0 %all-to-all-start.3 = ((bf16[32,128,256]{2,0,1:T(8,128)(2,1)}), bf16[32,128,256]{2,0,1:T(8,128)(2,1)S(1)}, u32[]{:S(2)}, u32[]{:S(2)}) async-start(bf16[32,128,256]{2,0,1:T(8,128)(2,1)} %copy.80), calls=%async_computation.3 | async-start | bytes 4194304 | tf_op jit(solution)/shard_map/all_to_all | solution.py:37
  177.8 0.6 slice_bitcast_fusion
  178.4 40.6 %all-gather.5.cloned.1.call-done = bf16[16384,256]{1,0:T(8,128)(2,1)} async-done(((bf16[128,256]{1,0:T(8,128)(2,1)}), bf16[16384,256]{1,0:T(8,128)(2,1)}) %all-gather.5.cloned.1.call-update) | async-done | bytes 8388624 | tf_op jit(solution)/shard_map/all_gather | solution.py:126
  219.0 9.9 %multiply_reduce_fusion = (f32[128]{0:T(128)S(1)}, f32[128,256]{1,0:T(8,128)S(1)}) fusion(f32[128,256]{1,0:T(8,128)S(1)} %get-tuple-element.17, f32[128]{0:T(128)S(1)} %add_rsqrt_fusion, bf16[16384,256]{1,0:T(8,128)(2,1)} %all-gather.5.cloned.1.call-done, bf16[128,256]{1,0:T(8,128)(2,1)} %multiply_convert_fusion, f32[16384]{0:T(1024)} %get-tuple-element.13, ...), kind=kOutput, calls=%fused_computation.77 | convolution fusion | flops 2162294784 | bytes 8848904 | tf_op jit(solution)/shard_map/dot_general | solution.py:167
  228.9 0.4 fusion.55
  229.5 0.4 convolution_convert_fusion
  230.2 1.2 pad_maximum_fusion.1
  231.5 6.0 %all-to-all-start.5 = ((bf16[6,128,256]{2,0,1:T(8,128)(2,1)}), bf16[6,128,256]{2,0,1:T(8,128)(2,1)S(1)}, u32[]{:S(2)}, u32[]{:S(2)}) async-start(bf16[6,128,256]{2,0,1:T(8,128)(2,1)} %pad_maximum_fusion.1), calls=%async_computation.5 | async-start | bytes 1048576 | tf_op jit(solution)/shard_map/all_to_all | solution.py:37
  237.5 1.2 slice_reduce_fusion
  238.7 2.5 copy.81
  241.2 10.3 %all-to-all-done.5 = bf16[6,128,256]{2,0,1:T(8,128)(2,1)S(1)} async-done(((bf16[6,128,256]{2,0,1:T(8,128)(2,1)}), bf16[6,128,256]{2,0,1:T(8,128)(2,1)S(1)}, u32[]{:S(2)}, u32[]{:S(2)}) %all-to-all-start.5) | async-done | bytes 393248 | tf_op jit(solution)/shard_map/all_to_all | solution.py:37
  251.9 0.9 broadcast_in_dim.55
  252.8 4.3 %all-to-all-start.6 = ((f32[4,128,256]{2,0,1:T(4,128)}), f32[4,128,256]{2,0,1:T(4,128)S(1)}, u32[]{:S(2)}, u32[]{:S(2)}) async-start(f32[4,128,256]{2,0,1:T(4,128)} %broadcast_in_dim.55), calls=%async_computation.6 | async-start | bytes 1048576 | tf_op jit(solution)/shard_map/all_to_all | solution.py:37
  257.1 14.9 %fusion = f32[4096,256]{1,0:T(8,128)} fusion(bf16[4096,256]{1,0:T(8,128)(2,1)} %bitcast.84, s32[4096]{0:T(1024)S(1)} %bitcast.106), kind=kOutput, calls=%fused_computation.2 | convolution fusion | flops 8606711808 | bytes 6307840 | tf_op jit(solution)/shard_map/dot_general | solution.py:33
  272.1 2.8 fusion.17
  275.1 0.7 copy.92
  275.9 0.7 copy.93
  (74 shorter events, 3.9 us)
Async XLA Ops:
  7.2 51.8 %copy-start = (bf16[4096,256]{1,0:T(8,128)(2,1)S(1)}, bf16[4096,256]{1,0:T(8,128)(2,1)}, u32[]{:S(2)}) copy-start(bf16[4096,256]{1,0:T(8,128)(2,1)} %param.12) | copy-start | bytes 6291460
  7.2 8.0 %copy-start.8 = (s32[2048,1]{0,1:T(1,128)S(1)}, s32[2048,1]{0,1:T(1,128)}, u32[]{:S(2)}) copy-start(s32[2048,1]{0,1:T(1,128)} %param.14) | copy-start | bytes 24580
  7.2 8.7 %copy-start.10 = (s32[128]{0:T(128)S(1)}, s32[128]{0:T(128)}, u32[]{:S(2)}) copy-start(s32[128]{0:T(128)} %param.20) | copy-start | bytes 1540
  7.2 8.7 %copy-start.9 = (s32[2048]{0:T(1024)S(1)}, s32[2048]{0:T(1024)}, u32[]{:S(2)}) copy-start(s32[2048]{0:T(1024)} %param.15) | copy-start | bytes 24580
  12.6 1.0 copy-start.4
  16.3 41.5 %copy-start.7 = (bf16[256,256]{1,0:T(8,128)(2,1)S(1)}, bf16[256,256]{1,0:T(8,128)(2,1)}, u32[]{:S(2)}) copy-start(bf16[256,256]{1,0:T(8,128)(2,1)} %param.22) | copy-start | bytes 393220
  18.5 21.2 %all-to-all-start = ((s32[34,128,1]{0,2,1:T(1,128)}), s32[34,128,1]{0,2,1:T(1,128)S(1)}, u32[]{:S(2)}, u32[]{:S(2)}) async-start(s32[34,128,1]{0,2,1:T(1,128)} %copy.72), calls=%async_computation | async-start | bytes 131072 | tf_op jit(solution)/shard_map/all_to_all | solution.py:37
  43.1 14.5 %all-to-all-start.2 = ((bf16[2,128,256]{2,0,1:T(2,128)(2,1)}), bf16[2,128,256]{2,0,1:T(2,128)(2,1)S(1)}, u32[]{:S(2)}, u32[]{:S(2)}) async-start(bf16[2,128,256]{2,0,1:T(2,128)(2,1)} %copy.77), calls=%async_computation.2 | async-start | bytes 262144 | tf_op jit(solution)/shard_map/all_to_all | solution.py:37
  47.4 88.1 %all-gather.3.cloned.1.call-start = ((), (), s32[]{:S(2)}) async-start(), calls=%async_computation.7 | async-start | bytes 8454144 | tf_op jit(solution)/shard_map/all_gather | solution.py:117
  71.2 7.1 %copy-start.11 = (bf16[64]{0:T(256)(128)(2,1)S(1)}, bf16[64]{0:T(256)(128)(2,1)}, u32[]{:S(2)}) copy-start(bf16[64]{0:T(256)(128)(2,1)} %param.18) | copy-start | bytes 388
  73.7 35.6 %all-to-all-start.1 = ((bf16[32,128,256]{2,0,1:T(8,128)(2,1)}), bf16[32,128,256]{2,0,1:T(8,128)(2,1)S(1)}, u32[]{:S(2)}, u32[]{:S(2)}) async-start(bf16[32,128,256]{2,0,1:T(8,128)(2,1)} %copy.74), calls=%async_computation.1 | async-start | bytes 4194304 | tf_op jit(solution)/shard_map/all_to_all | solution.py:37
  77.7 141.3 %all-gather.5.cloned.1.call-start = ((), (), s32[]{:S(2)}) async-start(), calls=%async_computation.8 | async-start | bytes 8454144 | tf_op jit(solution)/shard_map/all_gather | solution.py:126
  79.1 32.1 %copy-start.6 = (bf16[256,256]{1,0:T(8,128)(2,1)S(1)}, bf16[256,256]{1,0:T(8,128)(2,1)}, u32[]{:S(2)}) copy-start(bf16[256,256]{1,0:T(8,128)(2,1)} %param.21) | copy-start | bytes 393220
  141.8 3.4 %copy-start.3 = (bf16[16384,256]{1,0:T(8,128)(2,1)S(1)}, bf16[16384,256]{1,0:T(8,128)(2,1)}, u32[]{:S(2)}) copy-start(bf16[16384,256]{1,0:T(8,128)(2,1)} %all-gather.3.cloned.1.call-done) | copy-start | bytes 25165828
  150.4 2.0 copy-start.2
  154.2 19.4 %all-to-all-start.4 = ((f32[128,3,256]{2,1,0:T(4,128)}), f32[128,3,256]{2,1,0:T(4,128)S(1)}, u32[]{:S(2)}, u32[]{:S(2)}) async-start(f32[128,3,256]{2,1,0:T(4,128)} %pad_maximum_fusion), calls=%async_computation.4 | async-start | bytes 1048576 | tf_op jit(solution)/shard_map/all_to_all | solution.py:156
  173.6 55.3 %copy-start.5 = (f32[128,3,256]{2,1,0:T(4,128)}, f32[128,3,256]{2,1,0:T(4,128)S(1)}, u32[]{:S(2)}) copy-start(f32[128,3,256]{2,1,0:T(4,128)S(1)} %all-to-all-done.4) | copy-start | bytes 1179652
  173.6 57.9 %all-to-all-start.3 = ((bf16[32,128,256]{2,0,1:T(8,128)(2,1)}), bf16[32,128,256]{2,0,1:T(8,128)(2,1)S(1)}, u32[]{:S(2)}, u32[]{:S(2)}) async-start(bf16[32,128,256]{2,0,1:T(8,128)(2,1)} %copy.80), calls=%async_computation.3 | async-start | bytes 4194304 | tf_op jit(solution)/shard_map/all_to_all | solution.py:37
  231.5 20.1 %all-to-all-start.5 = ((bf16[6,128,256]{2,0,1:T(8,128)(2,1)}), bf16[6,128,256]{2,0,1:T(8,128)(2,1)S(1)}, u32[]{:S(2)}, u32[]{:S(2)}) async-start(bf16[6,128,256]{2,0,1:T(8,128)(2,1)} %pad_maximum_fusion.1), calls=%async_computation.5 | async-start | bytes 1048576 | tf_op jit(solution)/shard_map/all_to_all | solution.py:37
  252.8 22.1 %all-to-all-start.6 = ((f32[4,128,256]{2,0,1:T(4,128)}), f32[4,128,256]{2,0,1:T(4,128)S(1)}, u32[]{:S(2)}, u32[]{:S(2)}) async-start(f32[4,128,256]{2,0,1:T(4,128)} %broadcast_in_dim.55), calls=%async_computation.6 | async-start | bytes 1048576 | tf_op jit(solution)/shard_map/all_to_all | solution.py:37
  272.1 4.5 %copy-start.1 = (bf16[4096,256]{1,0:T(8,128)(2,1)S(1)}, bf16[4096,256]{1,0:T(8,128)(2,1)}, u32[]{:S(2)}) copy-start(bf16[4096,256]{1,0:T(8,128)(2,1)} %param.12) | copy-start | bytes 6291460
Sparse Core Ops, SparseCore 0:
  59.0 76.4 all-gather.2
  139.2 79.7 all-gather.4
where the time goes:
time: 289 us; the launch traced here: 284 us
  waiting for transfers between devices  130 us (45%)
  matrix products  57.4 us (20%)
  starting transfers between devices  40.4 us (14%)
  local copies, waits for them, and re-layouts  21.6 us (7%)
  other arithmetic  18.7 us (6%)
  between operations  15.5 us (5%)
    all_to_all x6, waiting for transfers between devices, exchange(): return lax.all_to_all(x, AXES, split_axis=1, concat_axis=1, tiled=True)  59.7 us
    all_gather x1, waiting for transfers between devices, local(): uh_all = lax.all_gather(uh, AXES, axis=0, tiled=True)  40.6 us
    all_to_all x6, starting transfers between devices, exchange(): return lax.all_to_all(x, AXES, split_axis=1, concat_axis=1, tiled=True)  34.1 us
    all_gather x1, waiting for transfers between devices, local(): vh_all = lax.all_gather(vh, AXES, axis=0, tiled=True)  22.4 us
    dot_general x2, matrix products, add_rows(): jnp.dot(onehot, values.reshape(flat.shape[0], -1), preferred_element_type...  17.7 us
    dot_general x2, matrix products, pick_rows(): jnp.dot(onehot, table, preferred_element_type=jnp.float32)  14.7 us
    dot_general x1, matrix products, local(): jnp.dot(pw_c, uh_all, preferred_element_type=jnp.float32)  9.92 us
    all_to_all x1, waiting for transfers between devices, local(): lax.all_to_all(jnp.concatenate([stats, user_parts], axis=1), AXES, split_...  7.28 us
  transfers between devices with their start and end apart: 9, of which 7 were waited for; matrix products, arithmetic and copies ran while one was open for 27% of the time, Pallas kernels for 0%

commit v1 on v0

--- a/solution.py
+++ b/solution.py
@@ -123,7 +123,10 @@
     bag = (numer / denom[:, None]).astype(jnp.bfloat16)
     un, ru = tower(bag, user_proj)
     uh = un.astype(jnp.bfloat16)
-    uh_all = lax.all_gather(uh, AXES, axis=0, tiled=True)
+    uh_all = jnp.concatenate(
+        lax.all_to_all(jnp.stack([uh for _ in range(lax.axis_size(AXES))], axis=0), AXES, 0, 0),
+        axis=0,
+    )
     scale = logit_scale[0]
     total = vh_all.shape[0]
     mine = myself * samples + sample_ids

time: 289 us -> 392 us (1.36)
  waiting for transfers between devices: 130 us -> 216 us
  blocking collectives: 0 us -> 19.2 us
  other arithmetic: 18.7 us -> 12.3 us
  starting transfers between devices: 40.4 us -> 44.7 us
    all_to_all x1, waiting for transfers between devices: 7.28 us -> 101 us  [local(): lax.all_to_all(jnp.stack([uh for _ in range(lax.axis_size(AXES))], axis=0...]
    all_gather x1 -> x0, waiting for transfers between devices: 40.6 us -> none  [local(): uh_all = lax.all_gather(uh, AXES, axis=0, tiled=True)]
    all_to_all x6, waiting for transfers between devices: 59.7 us -> 91.2 us  [exchange(): return lax.all_to_all(x, AXES, split_axis=1, concat_axis=1, tiled=True)]
    all_to_all x0 -> x1, blocking collectives: none -> 19.2 us  [local(): lax.all_to_all(jnp.concatenate([stats, user_parts], axis=1), AXES, split_...]
    all_to_all x6, starting transfers between devices: 34.1 us -> 38.6 us  [exchange(): return lax.all_to_all(x, AXES, split_axis=1, concat_axis=1, tiled=True)]
    another operation x3 -> x4, local copies, waits for them, and re-layouts: 0.35 us -> 4.6 us  [the longest x1 4.25 us: local(): jnp.stack([uh for _ in range(lax.axis_size(AXES))], axis=0)]
  transfers between devices with their start and end apart: 9 -> 8, of which waited for: 7 -> 8; matrix products, arithmetic and copies ran while one was open for 27% -> 8% of each run, Pallas kernels for 0% -> 0%
where the time goes in v1:
time: 392 us; the launch traced here: 387 us
  waiting for transfers between devices  216 us (55%)
  matrix products  55.7 us (14%)
  starting transfers between devices  44.7 us (11%)
  local copies, waits for them, and re-layouts  23.5 us (6%)
  blocking collectives  19.2 us (5%)
  between operations  15.6 us (4%)
  other arithmetic  12.3 us (3%)
    all_to_all x1, waiting for transfers between devices, local(): lax.all_to_all(jnp.stack([uh for _ in range(lax.axis_size(AXES))], axis=0...  101 us
    all_to_all x6, waiting for transfers between devices, exchange(): return lax.all_to_all(x, AXES, split_axis=1, concat_axis=1, tiled=True)  91.2 us
    all_to_all x6, starting transfers between devices, exchange(): return lax.all_to_all(x, AXES, split_axis=1, concat_axis=1, tiled=True)  38.6 us
    all_gather x1, waiting for transfers between devices, local(): vh_all = lax.all_gather(vh, AXES, axis=0, tiled=True)  24 us
    all_to_all x1, blocking collectives, local(): lax.all_to_all(jnp.concatenate([stats, user_parts], axis=1), AXES, split_...  19.2 us
    dot_general x2, matrix products, add_rows(): jnp.dot(onehot, values.reshape(flat.shape[0], -1), preferred_element_type...  16 us
    dot_general x2, matrix products, pick_rows(): jnp.dot(onehot, table, preferred_element_type=jnp.float32)  14.6 us
    dot_general x1, matrix products, local(): jnp.dot(pw_c, uh_all, preferred_element_type=jnp.float32)  9.88 us
  transfers between devices with their start and end apart: 8, of which 8 were waited for; matrix products, arithmetic and copies ran while one was open for 8% of the time, Pallas kernels for 0%

profile of v1, /device:TPU:1, one launch (start us, length us, event | category | flops | bytes accessed | tf_op | source)
XLA Modules:
  0.0 386.9 jit_solution(11842535581947616337)
XLA Ops:
  7.3 0.9 fusion.47
  8.3 0.8 select_reduce_fusion.1
  9.2 0.8 copy.70
  10.0 0.3 fusion.34
  10.4 0.3 copy.71
  10.8 0.6 fusion.33
  11.8 0.3 broadcast_multiply_fusion
  12.1 1.2 convolution_convert_fusion.1
  13.5 0.7 copy.72
  14.3 11.5 %all-to-all-start = ((s32[34,128,1]{0,2,1:T(1,128)}), s32[34,128,1]{0,2,1:T(1,128)S(1)}, u32[]{:S(2)}, u32[]{:S(2)}) async-start(s32[34,128,1]{0,2,1:T(1,128)} %copy.72), calls=%async_computation | async-start | bytes 131072 | tf_op jit(solution)/shard_map/all_to_all | solution.py:37
  25.8 9.7 %all-to-all-done = s32[34,128,1]{0,2,1:T(1,128)S(1)} async-done(((s32[34,128,1]{0,2,1:T(1,128)}), s32[34,128,1]{0,2,1:T(1,128)S(1)}, u32[]{:S(2)}, u32[]{:S(2)}) %all-to-all-start) | async-done | bytes 17440 | tf_op jit(solution)/shard_map/all_to_all | solution.py:37
  35.7 2.4 fusion.25
  38.1 0.8 copy.77
  38.9 4.3 %all-to-all-start.2 = ((bf16[2,128,256]{2,0,1:T(2,128)(2,1)}), bf16[2,128,256]{2,0,1:T(2,128)(2,1)S(1)}, u32[]{:S(2)}, u32[]{:S(2)}) async-start(bf16[2,128,256]{2,0,1:T(2,128)(2,1)} %copy.77), calls=%async_computation.2 | async-start | bytes 262144 | tf_op jit(solution)/shard_map/all_to_all | solution.py:37
  43.2 0.3 all-gather.2.cloned.1.call-start
  43.5 0.4 fusion.18
  43.9 9.5 %all-to-all-done.2 = bf16[2,128,256]{2,0,1:T(2,128)(2,1)S(1)} async-done(((bf16[2,128,256]{2,0,1:T(2,128)(2,1)}), bf16[2,128,256]{2,0,1:T(2,128)(2,1)S(1)}, u32[]{:S(2)}, u32[]{:S(2)}) %all-to-all-start.2) | async-done | bytes 131104 | tf_op jit(solution)/shard_map/all_to_all | solution.py:37
  53.6 0.3 multiply_reduce_fusion.2
  53.9 0.7 multiply_convert_fusion
  54.7 12.3 %fusion.11 = bf16[4096,256]{1,0:T(8,128)(2,1)S(1)} fusion(bf16[4096,256]{1,0:T(8,128)(2,1)S(1)} %copy-done, s32[4096]{0:T(1024)S(1)} %bitcast.106), kind=kOutput, calls=%fused_computation.18 | convolution fusion | flops 8607760384 | bytes 4210688 | tf_op jit(solution)/shard_map/dot_general | solution.py:26
  67.0 2.5 copy.74
  69.5 4.6 %all-to-all-start.1 = ((bf16[32,128,256]{2,0,1:T(8,128)(2,1)}), bf16[32,128,256]{2,0,1:T(8,128)(2,1)S(1)}, u32[]{:S(2)}, u32[]{:S(2)}) async-start(bf16[32,128,256]{2,0,1:T(8,128)(2,1)} %copy.74), calls=%async_computation.1 | async-start | bytes 4194304 | tf_op jit(solution)/shard_map/all_to_all | solution.py:37
  74.2 0.3 select_reduce_fusion
  75.1 0.5 convert_reduce_fusion
  75.7 30.0 %all-to-all-done.1 = bf16[32,128,256]{2,0,1:T(8,128)(2,1)S(1)} async-done(((bf16[32,128,256]{2,0,1:T(8,128)(2,1)}), bf16[32,128,256]{2,0,1:T(8,128)(2,1)S(1)}, u32[]{:S(2)}, u32[]{:S(2)}) %all-to-all-start.1) | async-done | bytes 2097184 | tf_op jit(solution)/shard_map/all_to_all | solution.py:37
  105.7 1.2 copy.75
  106.9 0.7 fusion.30
  107.5 0.3 multiply_reduce_fusion.3
  107.9 24.0 %all-gather.2.cloned.1.call-done = bf16[16384,256]{1,0:T(8,128)(2,1)} async-done(((bf16[128,256]{1,0:T(8,128)(2,1)}), bf16[16384,256]{1,0:T(8,128)(2,1)}) %all-gather.2.cloned.1.call-update) | async-done | bytes 8388624 | tf_op jit(solution)/shard_map/all_gather | solution.py:117
  131.9 6.3 %fusion.57 = (f32[128]{0:T(128)S(1)}, f32[128,16384]{1,0:T(8,128)S(1)}) fusion(bf16[128,256]{1,0:T(8,128)(2,1)S(1)} %multiply_convert_fusion.1, bf16[16384,256]{1,0:T(8,128)(2,1)} %all-gather.2.cloned.1.call-done, f32[]{:T(128)} %bitcast.79), kind=kOutput, calls=%fused_computation.123 | convolution fusion | flops 1077936000 | bytes 16843268 | tf_op jit(solution)/shard_map/dot_general | solution.py:134
  138.3 1.6 fusion.10
  139.8 1.8 copy-done.3
  141.6 2.9 multiply_reduce_fusion.1
  144.6 0.4 fusion.53
  145.2 0.2 pad_maximum_fusion
  145.5 19.2 %all_to_all.41 = f32[128,3,256]{2,1,0:T(4,128)S(1)} all-to-all(f32[128,3,256]{2,1,0:T(4,128)S(1)} %pad_maximum_fusion), channel_id=1, replica_groups=mesh['dp'=8,'table'=16] {'dp','table'}, dimensions={0} | all-to-all | bytes 786432 | tf_op jit(solution)/shard_map/all_to_all | solution.py:159
  164.7 4.3 %stack.11 = bf16[128,128,256]{2,1,0:T(8,128)(2,1)} broadcast(bf16[128,256]{1,0:T(8,128)(2,1)S(1)} %multiply_convert_fusion.1), dimensions={1,2} | broadcast | bytes 8454144 | tf_op jit(solution)/shard_map/stack | solution.py:127
  169.0 5.7 %all-to-all-start.4 = ((bf16[128,128,256]{2,1,0:T(8,128)(2,1)}), bf16[128,128,256]{2,1,0:T(8,128)(2,1)}, u32[]{:S(2)}, u32[]{:S(2)}) async-start(bf16[128,128,256]{2,1,0:T(8,128)(2,1)} %stack.11), calls=%async_computation.4 | async-start | bytes 16777216 | tf_op jit(solution)/shard_map/all_to_all | solution.py:127
  174.9 0.3 fusion.54
  175.3 100.6 %all-to-all-done.4 = bf16[128,128,256]{2,1,0:T(8,128)(2,1)} async-done(((bf16[128,128,256]{2,1,0:T(8,128)(2,1)}), bf16[128,128,256]{2,1,0:T(8,128)(2,1)}, u32[]{:S(2)}, u32[]{:S(2)}) %all-to-all-start.4) | async-done | bytes 8388640 | tf_op jit(solution)/shard_map/all_to_all | solution.py:127
  275.9 9.9 %multiply_reduce_fusion = (f32[128]{0:T(128)S(1)}, f32[128,256]{1,0:T(8,128)S(1)}) fusion(f32[128,256]{1,0:T(8,128)S(1)} %get-tuple-element.17, f32[128]{0:T(128)S(1)} %add_rsqrt_fusion, bf16[16384,256]{1,0:T(8,128)(2,1)} %bitcast.21, bf16[128,256]{1,0:T(8,128)(2,1)S(1)} %copy-done.5, f32[16384]{0:T(1024)S(1)} %get-tuple-element.13, ...), kind=kOutput, calls=%fused_computation.77 | convolution fusion | flops 2162294784 | bytes 8848904 | tf_op jit(solution)/shard_map/dot_general | solution.py:170
  285.8 0.4 convolution_convert_fusion
  286.2 0.4 fusion.55
  286.8 0.2 subtract_convert_fusion
  287.1 1.2 pad_maximum_fusion.1
  288.3 9.8 %all-to-all-start.6 = ((bf16[6,128,256]{2,0,1:T(8,128)(2,1)}), bf16[6,128,256]{2,0,1:T(8,128)(2,1)S(1)}, u32[]{:S(2)}, u32[]{:S(2)}) async-start(bf16[6,128,256]{2,0,1:T(8,128)(2,1)} %pad_maximum_fusion.1), calls=%async_computation.6 | async-start | bytes 1048576 | tf_op jit(solution)/shard_map/all_to_all | solution.py:37
  298.2 1.9 fusion.22
  300.2 2.0 copy-done.2
  302.2 0.2 slice_reduce_fusion
  302.4 9.9 %all-to-all-done.6 = bf16[6,128,256]{2,0,1:T(8,128)(2,1)S(1)} async-done(((bf16[6,128,256]{2,0,1:T(8,128)(2,1)}), bf16[6,128,256]{2,0,1:T(8,128)(2,1)S(1)}, u32[]{:S(2)}, u32[]{:S(2)}) %all-to-all-start.6) | async-done | bytes 393248 | tf_op jit(solution)/shard_map/all_to_all | solution.py:37
  312.4 0.2 fusion.40
  312.6 0.9 broadcast_in_dim.55
  313.5 4.0 %all-to-all-start.7 = ((f32[4,128,256]{2,0,1:T(4,128)}), f32[4,128,256]{2,0,1:T(4,128)S(1)}, u32[]{:S(2)}, u32[]{:S(2)}) async-start(f32[4,128,256]{2,0,1:T(4,128)} %broadcast_in_dim.55), calls=%async_computation.7 | async-start | bytes 1048576 | tf_op jit(solution)/shard_map/all_to_all | solution.py:37
  317.5 2.8 fusion.19
  320.3 0.5 copy.94
  320.8 3.4 copy.80
  324.3 7.4 %all-to-all-done.7 = f32[4,128,256]{2,0,1:T(4,128)S(1)} async-done(((f32[4,128,256]{2,0,1:T(4,128)}), f32[4,128,256]{2,0,1:T(4,128)S(1)}, u32[]{:S(2)}, u32[]{:S(2)}) %all-to-all-start.7) | async-done | bytes 524320 | tf_op jit(solution)/shard_map/all_to_all | solution.py:37
  331.7 4.4 %all-to-all-start.3 = ((bf16[32,128,256]{2,0,1:T(8,128)(2,1)}), bf16[32,128,256]{2,0,1:T(8,128)(2,1)S(1)}, u32[]{:S(2)}, u32[]{:S(2)}) async-start(bf16[32,128,256]{2,0,1:T(8,128)(2,1)} %copy.80), calls=%async_computation.3 | async-start | bytes 4194304 | tf_op jit(solution)/shard_map/all_to_all | solution.py:37
  336.2 2.8 fusion.17
  339.2 0.7 copy.92
  339.9 0.7 copy.93
  340.6 24.7 %all-to-all-done.3 = bf16[32,128,256]{2,0,1:T(8,128)(2,1)S(1)} async-done(((bf16[32,128,256]{2,0,1:T(8,128)(2,1)}), bf16[32,128,256]{2,0,1:T(8,128)(2,1)S(1)}, u32[]{:S(2)}, u32[]{:S(2)}) %all-to-all-start.3) | async-done | bytes 2097184 | tf_op jit(solution)/shard_map/all_to_all | solution.py:37
  365.3 1.2 copy.81
  366.5 13.2 %fusion = f32[4096,256]{1,0:T(8,128)} fusion(bf16[4096,256]{1,0:T(8,128)(2,1)S(1)} %bitcast.86, s32[4096]{0:T(1024)S(1)} %bitcast.107), kind=kOutput, calls=%fused_computation.2 | convolution fusion | flops 8606711808 | bytes 6307840 | tf_op jit(solution)/shard_map/dot_general | solution.py:33
  (77 shorter events, 2.9 us)
Async XLA Ops:
  7.2 47.5 %copy-start = (bf16[4096,256]{1,0:T(8,128)(2,1)S(1)}, bf16[4096,256]{1,0:T(8,128)(2,1)}, u32[]{:S(2)}) copy-start(bf16[4096,256]{1,0:T(8,128)(2,1)} %param.12) | copy-start | bytes 6291460
  7.2 3.6 copy-start.11
  7.2 3.6 copy-start.7
  7.2 4.3 %copy-start.9 = (s32[1,2048]{1,0:T(1,128)S(1)}, s32[1,2048]{1,0:T(1,128)}, u32[]{:S(2)}) copy-start(s32[1,2048]{1,0:T(1,128)} %param.16) | copy-start | bytes 24580
  7.2 4.4 %copy-start.10 = (s32[2048]{0:T(1024)S(1)}, s32[2048]{0:T(1024)}, u32[]{:S(2)}) copy-start(s32[2048]{0:T(1024)} %param.17) | copy-start | bytes 24580
  7.2 4.5 %copy-start.8 = (s32[2048]{0:T(1024)S(1)}, s32[2048]{0:T(1024)}, u32[]{:S(2)}) copy-start(s32[2048]{0:T(1024)} %param.15) | copy-start | bytes 24580
  7.2 4.5 %copy-start.12 = (s32[128]{0:T(128)S(1)}, s32[128]{0:T(128)}, u32[]{:S(2)}) copy-start(s32[128]{0:T(128)} %param.20) | copy-start | bytes 1540
  12.1 41.5 %copy-start.6 = (bf16[256,256]{1,0:T(8,128)(2,1)S(1)}, bf16[256,256]{1,0:T(8,128)(2,1)}, u32[]{:S(2)}) copy-start(bf16[256,256]{1,0:T(8,128)(2,1)} %param.22) | copy-start | bytes 393220
  14.3 21.2 %all-to-all-start = ((s32[34,128,1]{0,2,1:T(1,128)}), s32[34,128,1]{0,2,1:T(1,128)S(1)}, u32[]{:S(2)}, u32[]{:S(2)}) async-start(s32[34,128,1]{0,2,1:T(1,128)} %copy.72), calls=%async_computation | async-start | bytes 131072 | tf_op jit(solution)/shard_map/all_to_all | solution.py:37
  38.9 14.5 %all-to-all-start.2 = ((bf16[2,128,256]{2,0,1:T(2,128)(2,1)}), bf16[2,128,256]{2,0,1:T(2,128)(2,1)S(1)}, u32[]{:S(2)}, u32[]{:S(2)}) async-start(bf16[2,128,256]{2,0,1:T(2,128)(2,1)} %copy.77), calls=%async_computation.2 | async-start | bytes 262144 | tf_op jit(solution)/shard_map/all_to_all | solution.py:37
  43.2 88.7 %all-gather.2.cloned.1.call-start = ((), (), s32[]{:S(2)}) async-start(), calls=%async_computation.8 | async-start | bytes 8454144 | tf_op jit(solution)/shard_map/all_gather | solution.py:117
  67.0 7.2 %copy-start.13 = (bf16[64]{0:T(256)(128)(2,1)S(1)}, bf16[64]{0:T(256)(128)(2,1)}, u32[]{:S(2)}) copy-start(bf16[64]{0:T(256)(128)(2,1)} %param.18) | copy-start | bytes 388
  69.5 36.2 %all-to-all-start.1 = ((bf16[32,128,256]{2,0,1:T(8,128)(2,1)}), bf16[32,128,256]{2,0,1:T(8,128)(2,1)S(1)}, u32[]{:S(2)}, u32[]{:S(2)}) async-start(bf16[32,128,256]{2,0,1:T(8,128)(2,1)} %copy.74), calls=%async_computation.1 | async-start | bytes 4194304 | tf_op jit(solution)/shard_map/all_to_all | solution.py:37
  75.6 31.9 %copy-start.4 = (bf16[256,256]{1,0:T(8,128)(2,1)S(1)}, bf16[256,256]{1,0:T(8,128)(2,1)}, u32[]{:S(2)}) copy-start(bf16[256,256]{1,0:T(8,128)(2,1)} %param.21) | copy-start | bytes 393220
  138.2 3.4 copy-start.3
  169.0 107.0 %copy-start.5 = (bf16[128,256]{1,0:T(8,128)(2,1)S(1)}, bf16[128,256]{1,0:T(8,128)(2,1)}, u32[]{:S(2)}) copy-start(bf16[128,256]{1,0:T(8,128)(2,1)} %multiply_convert_fusion) | copy-start | bytes 196612
  169.0 107.0 %all-to-all-start.4 = ((bf16[128,128,256]{2,1,0:T(8,128)(2,1)}), bf16[128,128,256]{2,1,0:T(8,128)(2,1)}, u32[]{:S(2)}, u32[]{:S(2)}) async-start(bf16[128,128,256]{2,1,0:T(8,128)(2,1)} %stack.11), calls=%async_computation.4 | async-start | bytes 16777216 | tf_op jit(solution)/shard_map/all_to_all | solution.py:127
  288.3 23.9 %all-to-all-start.6 = ((bf16[6,128,256]{2,0,1:T(8,128)(2,1)}), bf16[6,128,256]{2,0,1:T(8,128)(2,1)S(1)}, u32[]{:S(2)}, u32[]{:S(2)}) async-start(bf16[6,128,256]{2,0,1:T(8,128)(2,1)} %pad_maximum_fusion.1), calls=%async_computation.6 | async-start | bytes 1048576 | tf_op jit(solution)/shard_map/all_to_all | solution.py:37
  300.2 2.0 copy-start.2
  313.5 18.2 %all-to-all-start.7 = ((f32[4,128,256]{2,0,1:T(4,128)}), f32[4,128,256]{2,0,1:T(4,128)S(1)}, u32[]{:S(2)}, u32[]{:S(2)}) async-start(f32[4,128,256]{2,0,1:T(4,128)} %broadcast_in_dim.55), calls=%async_computation.7 | async-start | bytes 1048576 | tf_op jit(solution)/shard_map/all_to_all | solution.py:37
  331.7 33.6 %all-to-all-start.3 = ((bf16[32,128,256]{2,0,1:T(8,128)(2,1)}), bf16[32,128,256]{2,0,1:T(8,128)(2,1)S(1)}, u32[]{:S(2)}, u32[]{:S(2)}) async-start(bf16[32,128,256]{2,0,1:T(8,128)(2,1)} %copy.80), calls=%async_computation.3 | async-start | bytes 4194304 | tf_op jit(solution)/shard_map/all_to_all | solution.py:37
  366.5 13.3 %copy-start.1 = (bf16[4096,256]{1,0:T(8,128)(2,1)S(1)}, bf16[4096,256]{1,0:T(8,128)(2,1)}, u32[]{:S(2)}) copy-start(bf16[4096,256]{1,0:T(8,128)(2,1)} %param.12) | copy-start | bytes 6291460
Sparse Core Ops, SparseCore 0:
  54.8 77.1 all-gather.1
